TPU v7x, 32 devices: a whole 2x2x4 slice. The times are simulated.
32 devices in a mesh: groups: 2 (over y), pipe: 4 (over z), dp: 2 (over x), mp: 2 (over core).
Axes of the slice: x: 2, y: 2, z: 4, core: 2. Of those that a mesh axis runs over, the one named last changes fastest.
Arguments:
- latent: bfloat16 [4, 2, 2, 4, 16, 320], P(('groups', 'dp')), parts along dimension 0, may hold values from -6 to 6
- section_weight: bfloat16 [4, 2, 921600], P('pipe', None, 'mp'), may hold values from -0.01613743 to 0.01613743, as said below
- out_grad: bfloat16 [4, 2, 2, 4, 16, 320], P(('groups', 'dp')), parts along dimension 0, may hold values from -0.29882812 to 0.29882812
Outputs:
- section_grad: float32 [8, 921600], P(('groups', 'pipe'), 'mp'), parts along dimension 0
There are 2 independent parts, one for each index of `groups`. A program takes and returns all parts, laid end to end along the dimension named above; an argument that names none is the same for every part. Nothing has to cross between parts.
Inputs may be any that keep to these rules, and one draw needn't show every extreme that they name: section_weight[j, 0] equals section_weight[3 - j, 0] and section_weight[j, 1] equals section_weight[3 - j, 1] for every j: both devices of a mirrored pair hold the same two blocks.
All inputs are finite; a program needn't handle non-finite values.
Results may differ from a plain program's by a relative error of at most 0.0065.
Values may be sent and summed in bfloat16 or wider, within the bound.
No kernel may reach another device: no remote copies, remote signals or barrier semaphores. Data moves between devices by JAX's collectives and lax.ppermute only.
A program may use at most 64 MiB of HBM per device.

v0:
```python
import jax
import jax.numpy as jnp
from jax import lax
from jax.sharding import PartitionSpec as P


def silu_slope(pre_act):
    sigmoid = jax.nn.sigmoid(pre_act)
    return sigmoid * (1.0 + pre_act * (1.0 - sigmoid))


def conv(act, weight):
    return lax.conv_general_dilated(
        act,
        weight,
        (1, 1),
        ((1, 1), (1, 1)),
        dimension_numbers=("NHWC", "OHWI", "NHWC"),
        preferred_element_type=jnp.float32,
    )


def conv_t(cot, weight):
    flipped = jnp.flip(cot, (1, 2))
    out = lax.conv_general_dilated(
        flipped,
        weight,
        (1, 1),
        ((1, 1), (1, 1)),
        dimension_numbers=("NHWC", "IHWO", "NHWC"),
        preferred_element_type=jnp.float32,
    )
    return jnp.flip(out, (1, 2))


def conv_flipped(flipped, weight):
    return lax.conv_general_dilated(
        flipped,
        weight,
        (1, 1),
        ((1, 1), (1, 1)),
        dimension_numbers=("NHWC", "IHWO", "NHWC"),
        preferred_element_type=jnp.float32,
    )


def weight_grad(act, cot):
    return lax.conv_general_dilated(
        act,
        cot,
        (1, 1),
        ((1, 1), (1, 1)),
        dimension_numbers=("CHWN", "IHWO", "CHWN"),
        preferred_element_type=jnp.float32,
    )


def f32(v):
    return v.astype(jnp.float32)


def bf16(v):
    return v.astype(jnp.bfloat16)


def on_stage(active, fn, *args):
    shapes = jax.eval_shape(fn, *args)

    def idle(*unused):
        return jax.tree.map(lambda v: jnp.zeros(v.shape, v.dtype), shapes)

    return lax.cond(active, fn, idle, *args)


def local(latent, section_weight, out_grad):
    pipe_size = lax.axis_size("pipe")
    half = pipe_size // 2
    device = lax.axis_index("pipe")
    lower = device < half
    stage = jnp.minimum(device, pipe_size - 1 - device)
    lane = lax.axis_index("mp")
    swap = [(0, 1), (1, 0)]
    channels = latent.shape[-1]
    img = latent.shape[-3:]
    samples = latent.reshape((-1,) + img)
    grads = out_grad.reshape((-1,) + img)
    per_lane = samples.shape[0] // 2
    mine = lane * per_lane
    theirs = (1 - lane) * per_lane
    chan_half = section_weight.shape[-1] // (9 * channels)
    own = lax.optimization_barrier(
        section_weight[0]
        .reshape(2, chan_half, 9, channels)
        .transpose(0, 2, 1, 3)
        .reshape(2, 3, 3, chan_half, channels)
    ).transpose(0, 3, 1, 2, 4)
    other = lax.ppermute(own, "mp", swap)

    def up(t, v):
        pairs = [(t, t + 1), (pipe_size - 1 - t, pipe_size - 2 - t)]
        return lax.ppermute(v, "pipe", pairs)

    def down(t, v):
        pairs = [(t, t - 1), (pipe_size - 1 - t, pipe_size - t)]
        return lax.ppermute(v, "pipe", pairs)

    def take(v, at):
        return lax.dynamic_slice_in_dim(v, at, per_lane, 0)

    def join(first, second):
        return jnp.where(
            lane == 0, jnp.concatenate([first, second], -1), jnp.concatenate([second, first], -1)
        )

    low = lane * chan_half
    high = (1 - lane) * chan_half
    x0 = take(samples, mine)
    seed = take(grads, mine)
    a0 = bf16(jax.nn.silu(f32(x0)))

    def first_own(a0, seed, own):
        flipped = jnp.flip(seed, (1, 2))
        d_own = conv_flipped(lax.dynamic_slice_in_dim(flipped, low, chan_half, 3), own[1])
        return (conv(a0, own[0]), d_own)

    def first_h1(x0, a0, other_enc, h1_own):
        return bf16(f32(x0) + join(h1_own, conv(a0, other_enc)))

    def first_d(seed, other_dec, d_own):
        flipped = jnp.flip(seed, (1, 2))
        d_other = conv_flipped(lax.dynamic_slice_in_dim(flipped, high, chan_half, 3), other_dec)
        return jnp.flip(d_own + d_other, (1, 2))

    h1_own, d_own = on_stage(stage == 0, first_own, a0, seed, own)
    h1 = on_stage(stage == 0, first_h1, x0, a0, other[0], h1_own)
    h1_r = up(0, h1)
    d_last = on_stage(stage == 0, first_d, seed, other[1], d_own)
    d_last_r = up(0, d_last)
    other, _ = lax.optimization_barrier((other, h1))
    full = jnp.where(lane == 0, jnp.concatenate([own, other], 1), jnp.concatenate([other, own], 1))
    w_enc, w_dec = (full[0], full[1])
    enc_in, enc_act, enc_out = ({}, {}, {})
    enc_in[0], enc_act[0], enc_out[0] = (x0, a0, h1)
    received = h1_r
    for t in range(1, half):
        h_in = received
        u = f32(h_in)
        a = bf16(jax.nn.silu(u))
        h_out = bf16(u + conv(a, w_enc))
        enc_in[t], enc_act[t], enc_out[t] = (h_in, a, h_out)
        if t < half - 1:
            received = up(t, h_out)
    dec_u, dec_act, dec_c = ({}, {}, {})
    h_in = enc_out[half - 1]
    u = f32(h_in) + f32(h_in)
    a = bf16(jax.nn.silu(u))
    current = bf16(f32(h_in) + conv(a, w_dec))
    dec_u[half - 1], dec_act[half - 1] = (u, a)
    for t in range(half - 2, 0, -1):
        h_in = down(t + 1, current)
        u = f32(h_in) + f32(enc_out[t])
        a = bf16(jax.nn.silu(u))
        current = bf16(f32(h_in) + conv(a, w_dec))
        dec_u[t], dec_act[t] = (u, a)
    u_last = f32(current) + f32(h1_r)
    a_last = bf16(jax.nn.silu(u_last))
    b_last = d_last_r * silu_slope(u_last)
    skip = {1: bf16(b_last)}
    cot = bf16(f32(seed) + b_last)
    for t in range(1, half):
        if t > 1:
            cot = up(t - 1, cot)
        dec_c[t] = cot
        d = conv_t(cot, w_dec)
        b = d * silu_slope(dec_u[t])
        g = bf16(f32(cot) + b)
        if t < half - 1:
            skip[t + 1] = bf16(b)
            cot = g
        else:
            cot = bf16(f32(g) + b)
    enc_c = {}
    for t in range(half - 1, 0, -1):
        if t < half - 1:
            cot = bf16(f32(down(t + 1, cot)) + f32(skip[t + 1]))
        enc_c[t] = cot
        d = conv_t(cot, w_enc)
        b = d * silu_slope(f32(enc_in[t]))
        cot = bf16(f32(cot) + b)
    c0 = bf16(f32(cot) + f32(skip[1]))
    sent = lax.ppermute(
        jnp.where(lower, c0, a_last), "pipe", [(1, 0), (pipe_size - 2, pipe_size - 1)]
    )
    acts_lo = jnp.stack([a0] + [enc_act[t] for t in range(1, half)])
    cots_lo = jnp.stack([sent] + [enc_c[t] for t in range(1, half)])
    acts_up = jnp.stack([sent] + [dec_act[t] for t in range(1, half)])
    cots_up = jnp.stack([seed] + [dec_c[t] for t in range(1, half)])
    act_sel = jnp.where(lower, acts_lo[stage], acts_up[stage])
    cot_sel = jnp.where(lower, cots_lo[stage], cots_up[stage])
    both = jnp.concatenate([act_sel, cot_sel], axis=-1)
    every = lax.all_gather(both, ("dp", "mp"), axis=0, tiled=True)
    act_all = every[..., :channels]
    cot_all = lax.dynamic_slice_in_dim(every, channels + low, chan_half, 3)
    grad = weight_grad(act_all, cot_all)
    return grad.reshape(1, -1)


def solution(mesh):
    return jax.shard_map(
        local,
        mesh=mesh,
        in_specs=(
            P(("groups", "dp"), None, None, None, None, None),
            P("pipe", None, "mp"),
            P(("groups", "dp"), None, None, None, None, None),
        ),
        out_specs=P(("groups", "pipe"), "mp"),
        check_vma=False,
    )
```

profile of v0, /device:TPU:0, one launch (start us, length us, event | category | flops | bytes accessed | tf_op | source)
XLA Modules:
  0.0 60.7 jit_solution(1006946981016055921)
XLA Ops:
  0.0 2.7 %reshape.100 = bf16[921600]{0:T(1024)(128)(2,1)S(1)} reshape(bf16[1,2,460800]{2,1,0:T(2,128)(2,1)} %param.10) | data formatting | bytes 3686400
  2.7 4.5 %reshape_squeeze.3 = bf16[2,160,9,320]{3,2,1,0:T(8,128)(2,1)} reshape(bf16[921600]{0:T(1024)(128)(2,1)S(1)} %reshape.100) | data formatting | bytes 3686400 | tf_op jit(solution)/shard_map/reshape;squeeze | solution.py:93
  7.1 2.7 %copy.72 = bf16[2,9,160,320]{3,2,1,0:T(8,128)(2,1)S(1)} copy(bf16[2,9,160,320]{3,1,2,0:T(8,128)(2,1)} %bitcast.129) | data formatting | bytes 3686400 | tf_op jit(solution)/shard_map/transpose | solution.py:94
  9.8 0.5 collective-permute-start
  10.6 0.1 fusion.67
  10.7 2.6 %conditional.3 = (f32[2,4,16,160]{3,1,2,0:T(4,128)S(1)}, f32[2,4,16,320]{3,1,2,0:T(4,128)S(1)}) conditional(s32[]{:T(128)} %convert_element_type.83, () %tuple.30, (bf16[2,160,3,3,320]{4,1,3,2,0:T(8,128)(2,1)S(1)}, bf16[2,4,16,320]{3,1,2,0:T(4,128)(2,1)S(1)}, bf16[2,4,16,320]{3,1,2,0:T(4,128)(2,1)S(1)}, s32[]{:T(128)}) %tuple.54), branch_computations={%region_0.1_spmd, %region_1.2_spmd} | conditional | flops 295925760 | bytes 5914902 | solution.py:72
  10.9 0.2 dynamic-slice_bitcast_fusion
  11.2 0.2 fusion.7
  11.7 0.2 fusion.4
  11.9 0.5 convolution_select_fusion.1
  12.5 0.5 convolution_select_fusion
  13.0 0.1 copy.66
  13.1 0.1 copy.64
  13.3 1.1 %collective-permute-done = bf16[2,160,3,3,320]{4,1,3,2,0:T(8,128)(2,1)} collective-permute-done((bf16[2,160,3,3,320]{4,1,3,2,0:T(8,128)(2,1)S(1)}, bf16[2,160,3,3,320]{4,1,3,2,0:T(8,128)(2,1)}, u32[]{:S(2)}, u32[]{:S(2)}) %collective-permute-start) | collective-permute-done | bytes 1843232 | tf_op jit(solution)/shard_map/ppermute | solution.py:97
  14.4 2.7 %conditional.4 = (bf16[2,4,16,320]{3,1,2,0:T(4,128)(2,1)S(1)}) conditional(s32[]{:T(128)} %convert_element_type.83, () %tuple.29, (bf16[2,4,16,320]{3,1,2,0:T(4,128)(2,1)S(1)}, s32[]{:T(128)}, bf16[2,160,3,3,320]{4,1,3,2,0:T(8,128)(2,1)}, bf16[2,4,16,320]{3,1,2,0:T(4,128)(2,1)S(1)}, f32[2,4,16,160]{3,1,2,0:T(4,128)S(1)}) %tuple.32), branch_computations={%region_2.3_spmd, %region_3.4_spmd} | conditional | flops 148346880 | bytes 3082772 | solution.py:72
  14.7 0.2 fusion.12
  14.9 1.8 %convolution_select_fusion.2 = f32[4,16,3,160]{3,1,2,0:T(8,128)S(1)} fusion(bf16[2,160,3,3,320]{4,1,3,2,0:T(8,128)(2,1)} %get-tuple-element.63, bf16[4,2,8,5,320]{4,1,3,2,0:T(2,128)(2,1)S(1)} %fusion.12, pred[16,3]{0,1:T(4,128)(4,1)} %constant.95), kind=kOutput, calls=%fused_computation.18 | convolution fusion | flops 147486720 | bytes 1434112 | tf_op jit(solution)/shard_map/cond/branch_1_fun/conv_general_dilated | solution.py:13
  16.7 0.1 copy.68
  16.9 0.2 fusion.16
  17.1 2.2 %collective-permute-start.1 = (bf16[2,4,16,320]{3,1,2,0:T(4,128)(2,1)S(1)}, bf16[2,4,16,320]{3,1,2,0:T(4,128)(2,1)S(1)}, u32[]{:S(2)}, u32[]{:S(2)}) collective-permute-start(bf16[2,4,16,320]{3,1,2,0:T(4,128)(2,1)S(1)} %get-tuple-element.119), channel_id=1, source_target_pairs={{0,4},{12,8},{1,5},{13,9},{2,6},{14,10},{3,7},{15,11},{16,20},{28,... | collective-permute-start | bytes 245768 | tf_op jit(solution)/shard_map/ppermute | solution.py:101
  19.3 3.0 %conditional.5 = (f32[2,4,16,320]{3,1,2,0:T(4,128)S(1)}) conditional(s32[]{:T(128)} %convert_element_type.83, () %tuple.33, (bf16[2,4,16,320]{3,1,2,0:T(4,128)(2,1)S(1)}, s32[]{:T(128)}, bf16[2,160,3,3,320]{4,1,3,2,0:T(8,128)(2,1)}, f32[2,4,16,320]{3,1,2,0:T(4,128)S(1)}) %tuple.34), branch_computations={%region_4.5_spmd, %region_5.6_spmd} | conditional | flops 147865600 | bytes 3548744 | solution.py:72
  19.5 0.1 dynamic-slice_bitcast_fusion.1
  19.8 0.2 fusion.20
  20.0 1.8 %convolution_select_fusion.3 = f32[4,16,3,320]{3,1,2,0:T(8,128)S(1)} fusion(bf16[2,160,3,3,320]{4,1,3,2,0:T(8,128)(2,1)} %get-tuple-element.67, bf16[4,2,8,5,160]{4,1,3,2,0:T(2,128)(2,1)S(1)} %fusion.20, pred[16,3]{0,1:T(4,128)(4,1)} %constant.94), kind=kOutput, calls=%fused_computation.30 | convolution fusion | flops 147517440 | bytes 1454592 | tf_op jit(solution)/shard_map/cond/branch_1_fun/conv_general_dilated | solution.py:37
  22.0 0.3 rev.20
  22.3 1.5 %collective-permute-start.2 = (f32[2,4,16,320]{3,1,2,0:T(4,128)S(1)}, f32[2,4,16,320]{3,1,2,0:T(4,128)S(1)}, u32[]{:S(2)}, u32[]{:S(2)}) collective-permute-start(f32[2,4,16,320]{3,1,2,0:T(4,128)S(1)} %get-tuple-element.120), channel_id=1, source_target_pairs={{0,4},{12,8},{1,5},{13,9},{2,6},{14,10},{3,7},{15,11},{16,20},{28,... | collective-permute-start | bytes 491528 | tf_op jit(solution)/shard_map/ppermute | solution.py:101
  23.8 3.6 %maximum_select_fusion.1 = bf16[2,320,3,3,320]{4,1,3,2,0:T(8,128)(2,1)S(1)} fusion(bf16[2,160,3,3,320]{4,1,3,2,0:T(8,128)(2,1)} %collective-permute-done, bf16[2,160,3,3,320]{4,1,3,2,0:T(8,128)(2,1)S(1)} %bitcast.132, pred[]{:T(512)S(6)} %eq.12), kind=kLoop, calls=%fused_computation.40 | loop fusion | flops 16588800 | bytes 7372801 | tf_op jit(solution)/shard_map/jit(_where)/select_n | solution.py:140
  27.7 1.0 %fusion.29 = f32[4,16,3,320]{3,1,2,0:T(8,128)S(1)} fusion(bf16[2,320,3,3,320]{4,1,3,2,0:T(8,128)(2,1)S(1)} %maximum_select_fusion.1, bf16[4,2,7,2,320]{4,2,1,3,0:T(8,128)(2,1)S(1)} %slice.51, bf16[4,2,8,3,320]{4,2,1,3,0:T(8,128)(2,1)S(1)} %copy.79, pred[16,3]{0,1:T(4,128)(4,1)S(1)} %copy-done.3), kind=kOutput, calls=%fused_computation.49 | convolution fusion | flops 295587840 | bytes 2703872 | tf_op jit(solution)/shard_map/conv_general_dilated | solution.py:13
  28.8 0.1 fusion.71
  29.1 1.0 %fusion.27 = f32[4,16,3,320]{3,1,2,0:T(8,128)S(1)} fusion(bf16[2,320,3,3,320]{4,1,3,2,0:T(8,128)(2,1)S(1)} %maximum_select_fusion.1, bf16[4,2,7,2,320]{4,2,1,3,0:T(8,128)(2,1)S(1)} %slice.54, bf16[4,2,8,3,320]{4,2,1,3,0:T(8,128)(2,1)S(1)} %copy.82, pred[16,3]{0,1:T(4,128)(4,1)S(1)} %copy-done.3), kind=kOutput, calls=%fused_computation.47 | convolution fusion | flops 295587840 | bytes 2703872 | tf_op jit(solution)/shard_map/conv_general_dilated | solution.py:13
  30.3 0.2 add_convert_fusion.3
  30.5 0.3 rev.25
  30.9 2.4 %fusion.28 = f32[4,16,3,320]{3,1,2,0:T(8,128)S(1)} fusion(bf16[2,320,3,3,320]{4,1,3,2,0:T(8,128)(2,1)} %copy-done, bf16[4,2,7,2,320]{4,2,1,3,0:T(8,128)(2,1)S(1)} %slice.57, bf16[4,2,8,3,320]{4,2,1,3,0:T(8,128)(2,1)S(1)} %copy.85, pred[16,3]{0,1:T(4,128)(4,1)S(1)} %copy-done.3), kind=kOutput, calls=%fused_computation.48 | convolution fusion | flops 295587840 | bytes 2652208 | tf_op jit(solution)/shard_map/conv_general_dilated | solution.py:25
  33.5 0.3 rev.26
  33.8 0.2 add_convert_fusion.1
  34.0 0.3 rev.27
  34.5 2.4 %fusion.30 = f32[4,16,3,320]{3,1,2,0:T(8,128)S(1)} fusion(bf16[2,320,3,3,320]{4,1,3,2,0:T(8,128)(2,1)} %copy-done, bf16[4,2,7,2,320]{4,2,1,3,0:T(8,128)(2,1)S(1)} %slice.59, bf16[4,2,8,3,320]{4,2,1,3,0:T(8,128)(2,1)S(1)} %copy.88, pred[16,3]{0,1:T(4,128)(4,1)S(1)} %copy-done.3), kind=kOutput, calls=%fused_computation.50 | convolution fusion | flops 295587840 | bytes 2652208 | tf_op jit(solution)/shard_map/conv_general_dilated | solution.py:25
  37.0 0.3 rev.28
  37.3 0.3 fusion.90
  37.7 1.3 %collective-permute-start.3 = (bf16[2,4,16,320]{3,1,2,0:T(4,128)(2,1)S(1)}, bf16[2,4,16,320]{3,1,2,0:T(4,128)(2,1)S(1)}, u32[]{:S(2)}, u32[]{:S(2)}) collective-permute-start(bf16[2,4,16,320]{3,1,2,0:T(4,128)(2,1)S(1)} %fusion.90), channel_id=1, source_target_pairs={{4,0},{8,12},{5,1},{9,13},{6,2},{10,14},{7,3},{11,15},{20,16},{24,... | collective-permute-start | bytes 245768 | tf_op jit(solution)/shard_map/ppermute | solution.py:191
  39.1 5.1 %collective-permute-done.3 = bf16[2,4,16,320]{3,1,2,0:T(4,128)(2,1)S(1)} collective-permute-done((bf16[2,4,16,320]{3,1,2,0:T(4,128)(2,1)S(1)}, bf16[2,4,16,320]{3,1,2,0:T(4,128)(2,1)S(1)}, u32[]{:S(2)}, u32[]{:S(2)}) %collective-permute-start.3) | collective-permute-done | bytes 81952 | tf_op jit(solution)/shard_map/ppermute | solution.py:191
  44.2 0.4 fusion.97
  44.6 0.1 pad_maximum_fusion
  44.8 8.8 %all_gather.3 = bf16[8,4,16,640]{3,2,1,0:T(8,128)(2,1)S(1)} all-gather(bf16[2,4,16,640]{3,2,1,0:T(8,128)(2,1)S(1)} %copy.90), channel_id=1, replica_groups=mesh['groups'=2,'pipe'=4,'dp'=2,'mp'=2] {'dp','mp'}, dimensions={0}, use_global_device_ids=true | all-gather | bytes 819200 | tf_op jit(solution)/shard_map/all_gather | solution.py:201
  53.6 0.2 constant_dynamic-slice_fusion
  53.8 0.9 %fusion.35 = f32[160,3,3,320]{3,0,2,1:T(8,128)S(1)} fusion(bf16[8,4,16,320]{3,2,1,0:T(8,128)(2,1)S(1)} %slice.61, bf16[8,4,16,160]{3,2,1,0:T(8,128)(2,1)S(1)} %constant_dynamic-slice_fusion), kind=kOutput, calls=%fused_computation.56 | convolution fusion | flops 376832000 | bytes 2334720 | tf_op jit(solution)/shard_map/conv_general_dilated | solution.py:48
  54.6 1.5 %copy.93 = f32[160,3,3,320]{3,2,1,0:T(4,128)S(1)} copy(f32[160,3,3,320]{3,0,2,1:T(8,128)S(1)} %fusion.35) | data formatting | bytes 3686400 | tf_op jit(solution)/shard_map/conv_general_dilated | solution.py:48
  56.2 4.6 %reshape.19 = f32[1,460800]{1,0:T(1,128)} reshape(f32[160,3,3,320]{3,2,1,0:T(4,128)S(1)} %copy.93) | data formatting | bytes 3686400 | tf_op jit(solution)/shard_map/reshape | solution.py:205
  (57 shorter events, 2.8 us)
Async XLA Ops:
  7.1 3.2 %copy-start.1 = (bf16[1,2,2,4,16,320]{5,4,3,2,1,0:T(8,128)(2,1)S(1)}, bf16[1,2,2,4,16,320]{5,4,3,2,1,0:T(8,128)(2,1)}, u32[]{:S(2)}) copy-start(bf16[1,2,2,4,16,320]{5,4,3,2,1,0:T(8,128)(2,1)} %param.9) | copy-start | bytes 491524
  7.1 3.3 %copy-start.2 = (bf16[1,2,2,4,16,320]{5,4,3,2,1,0:T(8,128)(2,1)S(1)}, bf16[1,2,2,4,16,320]{5,4,3,2,1,0:T(8,128)(2,1)}, u32[]{:S(2)}) copy-start(bf16[1,2,2,4,16,320]{5,4,3,2,1,0:T(8,128)(2,1)} %param.11) | copy-start | bytes 491524
  9.8 4.6 %collective-permute-start = (bf16[2,160,3,3,320]{4,1,3,2,0:T(8,128)(2,1)S(1)}, bf16[2,160,3,3,320]{4,1,3,2,0:T(8,128)(2,1)}, u32[]{:S(2)}, u32[]{:S(2)}) collective-permute-start(bf16[2,160,3,3,320]{4,1,3,2,0:T(8,128)(2,1)S(1)} %bitcast.130), channel_id=1, source_target_pairs={{0,1},{1,0},{2,3},{3,2},{4,5},{5,4},{6,7},{7,6},{8,9},{9,8},{10,11... | collective-permute-start | bytes 5529608 | tf_op jit(solution)/shard_map/ppermute | solution.py:97
  10.7 1.2 %copy-start.4 = (pred[16,3]{0,1:T(4,128)(4,1)S(1)}, pred[16,3]{0,1:T(4,128)(4,1)}, u32[]{:S(2)}) copy-start(pred[16,3]{0,1:T(4,128)(4,1)} %constant.96) | copy-start | bytes 148 | tf_op jit(solution)/shard_map/cond
  17.1 10.3 %collective-permute-start.1 = (bf16[2,4,16,320]{3,1,2,0:T(4,128)(2,1)S(1)}, bf16[2,4,16,320]{3,1,2,0:T(4,128)(2,1)S(1)}, u32[]{:S(2)}, u32[]{:S(2)}) collective-permute-start(bf16[2,4,16,320]{3,1,2,0:T(4,128)(2,1)S(1)} %get-tuple-element.119), channel_id=1, source_target_pairs={{0,4},{12,8},{1,5},{13,9},{2,6},{14,10},{3,7},{15,11},{16,20},{28,... | collective-permute-start | bytes 245768 | tf_op jit(solution)/shard_map/ppermute | solution.py:101
  22.3 5.4 %copy-start.3 = (pred[16,3]{0,1:T(4,128)(4,1)S(1)}, pred[16,3]{0,1:T(4,128)(4,1)}, u32[]{:S(2)}) copy-start(pred[16,3]{0,1:T(4,128)(4,1)} %constant.90) | copy-start | bytes 148
  22.3 8.0 %collective-permute-start.2 = (f32[2,4,16,320]{3,1,2,0:T(4,128)S(1)}, f32[2,4,16,320]{3,1,2,0:T(4,128)S(1)}, u32[]{:S(2)}, u32[]{:S(2)}) collective-permute-start(f32[2,4,16,320]{3,1,2,0:T(4,128)S(1)} %get-tuple-element.120), channel_id=1, source_target_pairs={{0,4},{12,8},{1,5},{13,9},{2,6},{14,10},{3,7},{15,11},{16,20},{28,... | collective-permute-start | bytes 491528 | tf_op jit(solution)/shard_map/ppermute | solution.py:101
  27.4 2.7 %copy-start = (bf16[2,320,3,3,320]{4,1,3,2,0:T(8,128)(2,1)}, bf16[2,320,3,3,320]{4,1,3,2,0:T(8,128)(2,1)S(1)}, u32[]{:S(2)}) copy-start(bf16[2,320,3,3,320]{4,1,3,2,0:T(8,128)(2,1)S(1)} %maximum_select_fusion.1) | copy-start | bytes 11059204
  37.7 6.5 %collective-permute-start.3 = (bf16[2,4,16,320]{3,1,2,0:T(4,128)(2,1)S(1)}, bf16[2,4,16,320]{3,1,2,0:T(4,128)(2,1)S(1)}, u32[]{:S(2)}, u32[]{:S(2)}) collective-permute-start(bf16[2,4,16,320]{3,1,2,0:T(4,128)(2,1)S(1)} %fusion.90), channel_id=1, source_target_pairs={{4,0},{8,12},{5,1},{9,13},{6,2},{10,14},{7,3},{11,15},{20,16},{24,... | collective-permute-start | bytes 245768 | tf_op jit(solution)/shard_map/ppermute | solution.py:191
where the time goes:
time: 61.1 us; the launch traced here: 60.7 us
  local copies, waits for them, and re-layouts  20.8 us (34%)
  matrix products  12.3 us (20%)
  blocking collectives  8.79 us (14%)
  other arithmetic  6.47 us (11%)
  waiting for transfers between devices  6.18 us (10%)
  starting transfers between devices  5.49 us (9%)
    all_gather x1, blocking collectives, local(): every = lax.all_gather(both, ('dp', 'mp'), axis=0, tiled=True)  8.79 us
    ppermute x1, waiting for transfers between devices, local(): lax.ppermute(jnp.where(lower, c0, a_last), 'pipe', [(1, 0), (pipe_size -...  5.09 us
    conv_general_dilated x2, matrix products, conv_t(): lax.conv_general_dilated(flipped, weight, (1, 1), ((1, 1), (1, 1)), dimen...  4.76 us
    reshape x1, local copies, waits for them, and re-layouts, local(): return grad.reshape(1, -1)  4.57 us
    another operation x1, local copies, waits for them, and re-layouts, local(): own = lax.optimization_barrier(section_weight[0].reshape(2, chan_half, 9,...  4.47 us
    conv_general_dilated x4, matrix products, conv(): lax.conv_general_dilated(act, weight, (1, 1), ((1, 1), (1, 1)), dimension...  4.36 us
    ppermute x2, starting transfers between devices, up(): return lax.ppermute(v, 'pipe', pairs)  3.68 us
    select_n x1, other arithmetic, local(): jnp.where(lane == 0, jnp.concatenate([own, other], 1), jnp.concatenate([o...  3.6 us
  transfers between devices with their start and end apart: 4, of which 2 were waited for; matrix products, arithmetic and copies ran while one was open for 20% of the time, Pallas kernels for 0%

commit v1 on v0

--- a/solution.py
+++ b/solution.py
@@ -2,6 +2,18 @@
 import jax.numpy as jnp
 from jax import lax
 from jax.sharding import PartitionSpec as P
+
+
+def gather_around(value, axis, dim):
+    ways, here, hop = (lax.axis_size(axis), lax.axis_index(axis), value.shape[dim])
+    shape = [n * ways if d == dim else n for d, n in enumerate(value.shape)]
+    full = lax.dynamic_update_slice_in_dim(
+        jnp.zeros(shape, value.dtype), value, here * hop, axis=dim
+    )
+    for far in range(1, ways):
+        value = lax.ppermute(value, axis, [(d, (d + 1) % ways) for d in range(ways)])
+        full = lax.dynamic_update_slice_in_dim(full, value, (here - far) % ways * hop, axis=dim)
+    return full
 
 
 def silu_slope(pre_act):
@@ -198,7 +210,7 @@
     act_sel = jnp.where(lower, acts_lo[stage], acts_up[stage])
     cot_sel = jnp.where(lower, cots_lo[stage], cots_up[stage])
     both = jnp.concatenate([act_sel, cot_sel], axis=-1)
-    every = lax.all_gather(both, ("dp", "mp"), axis=0, tiled=True)
+    every = gather_around(both, ("dp", "mp"), 0)
     act_all = every[..., :channels]
     cot_all = lax.dynamic_slice_in_dim(every, channels + low, chan_half, 3)
     grad = weight_grad(act_all, cot_all)

time: 61.1 us -> 66.9 us (1.095)
  waiting for transfers between devices: 6.18 us -> 19.1 us
  blocking collectives: 8.79 us -> 0 us
  local copies, waits for them, and re-layouts: 20.8 us -> 21.6 us
  matrix products: 12.3 us -> 13 us
    ppermute x0 -> x3, waiting for transfers between devices: none -> 13.3 us  [gather_around(): lax.ppermute(value, axis, [(d, (d + 1) % ways) for d in range(ways)])]
    all_gather x1 -> x0, blocking collectives: 8.79 us -> none  [local(): every = lax.all_gather(both, ('dp', 'mp'), axis=0, tiled=True)]
    dynamic_update_slice x0 -> x4, local copies, waits for them, and re-layouts: none -> 1.13 us  [the longest x3 0.84 us: gather_around(): lax.dynamic_update_slice_in_dim(full, value, (here - far) % ways * hop, a...]
    conv_general_dilated x2, matrix products: 2.28 us -> 3.02 us  [conv_flipped(): lax.conv_general_dilated(flipped, weight, (1, 1), ((1, 1), (1, 1)), dimen...]
    unnamed x11 -> x15, local copies, waits for them, and re-layouts: 2.84 us -> 3.13 us
  transfers between devices with their start and end apart: 4 -> 7, of which waited for: 2 -> 5; matrix products, arithmetic and copies ran while one was open for 20% -> 21% of each run, Pallas kernels for 0% -> 0%
where the time goes in v1:
time: 66.9 us; the launch traced here: 66.6 us
  local copies, waits for them, and re-layouts  21.6 us (32%)
  waiting for transfers between devices  19.1 us (29%)
  matrix products  13 us (19%)
  other arithmetic  6.46 us (10%)
  starting transfers between devices  5.55 us (8%)
    ppermute x3, waiting for transfers between devices, gather_around(): lax.ppermute(value, axis, [(d, (d + 1) % ways) for d in range(ways)])  13.3 us
    ppermute x1, waiting for transfers between devices, local(): lax.ppermute(jnp.where(lower, c0, a_last), 'pipe', [(1, 0), (pipe_size -...  5.18 us
    conv_general_dilated x2, matrix products, conv_t(): lax.conv_general_dilated(flipped, weight, (1, 1), ((1, 1), (1, 1)), dimen...  4.76 us
    reshape x1, local copies, waits for them, and re-layouts, local(): return grad.reshape(1, -1)  4.57 us
    another operation x1, local copies, waits for them, and re-layouts, local(): own = lax.optimization_barrier(section_weight[0].reshape(2, chan_half, 9,...  4.44 us
    conv_general_dilated x4, matrix products, conv(): lax.conv_general_dilated(act, weight, (1, 1), ((1, 1), (1, 1)), dimension...  4.35 us
    ppermute x2, starting transfers between devices, up(): return lax.ppermute(v, 'pipe', pairs)  3.68 us
    select_n x1, other arithmetic, local(): jnp.where(lane == 0, jnp.concatenate([own, other], 1), jnp.concatenate([o...  3.57 us
  transfers between devices with their start and end apart: 7, of which 5 were waited for; matrix products, arithmetic and copies ran while one was open for 21% of the time, Pallas kernels for 0%

profile of v1, /device:TPU:0, one launch (start us, length us, event | category | flops | bytes accessed | tf_op | source)
XLA Modules:
  0.0 66.6 jit_solution(18442952312014087435)
XLA Ops:
  0.0 2.7 %reshape.100 = bf16[921600]{0:T(1024)(128)(2,1)S(1)} reshape(bf16[1,2,460800]{2,1,0:T(2,128)(2,1)} %param.10) | data formatting | bytes 3686400
  2.7 4.4 %reshape_squeeze.3 = bf16[2,160,9,320]{3,2,1,0:T(8,128)(2,1)} reshape(bf16[921600]{0:T(1024)(128)(2,1)S(1)} %reshape.100) | data formatting | bytes 3686400 | tf_op jit(solution)/shard_map/reshape;squeeze | solution.py:105
  7.1 2.7 %copy.104 = bf16[2,9,160,320]{3,2,1,0:T(8,128)(2,1)S(1)} copy(bf16[2,9,160,320]{3,1,2,0:T(8,128)(2,1)} %bitcast.136) | data formatting | bytes 3686400 | tf_op jit(solution)/shard_map/transpose | solution.py:106
  9.8 0.5 collective-permute-start
  10.4 3.3 %conditional.3 = (f32[2,4,16,160]{3,1,2,0:T(4,128)S(1)}, f32[2,4,16,320]{3,1,2,0:T(4,128)S(1)}) conditional(s32[]{:T(128)} %convert_element_type.83, () %tuple.30, (bf16[2,160,3,3,320]{4,1,3,2,0:T(8,128)(2,1)S(1)}, bf16[2,4,16,320]{3,2,1,0:T(8,128)(2,1)S(1)}, bf16[2,4,16,320]{3,2,1,0:T(8,128)(2,1)S(1)}, s32[]{:T(128)}) %tuple.56), branch_computations={%region_0.1_spmd, %region_1.2_spmd} | conditional | flops 295925760 | bytes 5914438 | solution.py:84
  10.6 0.2 dynamic-slice_bitcast_fusion
  10.9 0.2 fusion.7
  11.1 1.2 %convolution_select_fusion = f32[4,16,3,320]{3,1,2,0:T(8,128)S(1)} fusion(bf16[2,160,3,3,320]{4,1,3,2,0:T(8,128)(2,1)S(1)} %get-tuple-element.56, bf16[4,2,8,5,160]{4,1,3,2,0:T(2,128)(2,1)S(1)} %fusion.7, pred[16,3]{0,1:T(4,128)(4,1)} %constant.125), kind=kOutput, calls=%fused_computation | convolution fusion | flops 147517440 | bytes 1515568 | tf_op jit(solution)/shard_map/cond/branch_1_fun/conv_general_dilated | solution.py:49
  12.8 0.2 fusion.4
  13.0 0.5 convolution_select_fusion.1
  13.6 0.1 copy.97
  13.7 0.7 collective-permute-done
  14.4 2.7 %conditional.4 = (bf16[2,4,16,320]{3,1,2,0:T(4,128)(2,1)S(1)}) conditional(s32[]{:T(128)} %convert_element_type.83, () %tuple.29, (bf16[2,4,16,320]{3,2,1,0:T(8,128)(2,1)S(1)}, s32[]{:T(128)}, bf16[2,160,3,3,320]{4,1,3,2,0:T(8,128)(2,1)}, bf16[2,4,16,320]{3,2,1,0:T(8,128)(2,1)S(1)}, f32[2,4,16,160]{3,1,2,0:T(4,128)S(1)}) %tuple.32), branch_computations={%region_2.3_spmd, %region_3.4_spmd} | conditional | flops 148346880 | bytes 3082772 | solution.py:84
  14.7 0.2 fusion.12
  14.9 1.8 %convolution_select_fusion.2 = f32[4,16,3,160]{3,1,2,0:T(8,128)S(1)} fusion(bf16[2,160,3,3,320]{4,1,3,2,0:T(8,128)(2,1)} %get-tuple-element.63, bf16[4,2,8,5,320]{4,1,3,2,0:T(2,128)(2,1)S(1)} %fusion.12, pred[16,3]{0,1:T(4,128)(4,1)} %constant.124), kind=kOutput, calls=%fused_computation.18 | convolution fusion | flops 147486720 | bytes 1434112 | tf_op jit(solution)/shard_map/cond/branch_1_fun/conv_general_dilated | solution.py:25
  16.9 0.2 fusion.16
  17.1 2.2 %collective-permute-start.1 = (bf16[2,4,16,320]{3,2,1,0:T(8,128)(2,1)S(1)}, bf16[2,4,16,320]{3,2,1,0:T(8,128)(2,1)S(1)}, u32[]{:S(2)}, u32[]{:S(2)}) collective-permute-start(bf16[2,4,16,320]{3,2,1,0:T(8,128)(2,1)S(1)} %copy.109), channel_id=1, source_target_pairs={{0,4},{12,8},{1,5},{13,9},{2,6},{14,10},{3,7},{15,11},{16,20},{28,... | collective-permute-start | bytes 245768 | tf_op jit(solution)/shard_map/ppermute | solution.py:113
  19.3 3.0 %conditional.5 = (f32[2,4,16,320]{3,1,2,0:T(4,128)S(1)}) conditional(s32[]{:T(128)} %convert_element_type.83, () %tuple.33, (bf16[2,4,16,320]{3,2,1,0:T(8,128)(2,1)S(1)}, s32[]{:T(128)}, bf16[2,160,3,3,320]{4,1,3,2,0:T(8,128)(2,1)}, f32[2,4,16,320]{3,1,2,0:T(4,128)S(1)}) %tuple.34), branch_computations={%region_4.5_spmd, %region_5.6_spmd} | conditional | flops 147865600 | bytes 3548744 | solution.py:84
  19.5 0.1 dynamic-slice_bitcast_fusion.1
  19.8 0.2 fusion.20
  20.0 1.8 %convolution_select_fusion.3 = f32[4,16,3,320]{3,1,2,0:T(8,128)S(1)} fusion(bf16[2,160,3,3,320]{4,1,3,2,0:T(8,128)(2,1)} %get-tuple-element.67, bf16[4,2,8,5,160]{4,1,3,2,0:T(2,128)(2,1)S(1)} %fusion.20, pred[16,3]{0,1:T(4,128)(4,1)} %constant.123), kind=kOutput, calls=%fused_computation.30 | convolution fusion | flops 147517440 | bytes 1454592 | tf_op jit(solution)/shard_map/cond/branch_1_fun/conv_general_dilated | solution.py:49
  22.0 0.3 rev.20
  22.3 1.5 %collective-permute-start.2 = (f32[2,4,16,320]{3,2,1,0:T(8,128)S(1)}, f32[2,4,16,320]{3,2,1,0:T(8,128)S(1)}, u32[]{:S(2)}, u32[]{:S(2)}) collective-permute-start(f32[2,4,16,320]{3,2,1,0:T(8,128)S(1)} %copy.111), channel_id=1, source_target_pairs={{0,4},{12,8},{1,5},{13,9},{2,6},{14,10},{3,7},{15,11},{16,20},{28,... | collective-permute-start | bytes 491528 | tf_op jit(solution)/shard_map/ppermute | solution.py:113
  23.8 3.6 %maximum_select_fusion.1 = bf16[2,320,3,3,320]{4,1,3,2,0:T(8,128)(2,1)S(1)} fusion(bf16[2,160,3,3,320]{4,1,3,2,0:T(8,128)(2,1)} %collective-permute-done, bf16[2,160,3,3,320]{4,1,3,2,0:T(8,128)(2,1)S(1)} %bitcast.139, pred[]{:T(512)S(6)} %eq.16), kind=kLoop, calls=%fused_computation.40 | loop fusion | flops 16588800 | bytes 7372801 | tf_op jit(solution)/shard_map/jit(_where)/select_n | solution.py:152
  27.8 0.2 fusion.38
  28.0 1.0 %fusion.29 = f32[4,16,3,320]{3,1,2,0:T(8,128)S(1)} fusion(bf16[2,320,3,3,320]{4,1,3,2,0:T(8,128)(2,1)S(1)} %maximum_select_fusion.1, bf16[4,2,8,5,320]{4,1,3,2,0:T(2,128)(2,1)S(1)} %fusion.38, pred[16,3]{0,1:T(4,128)(4,1)S(1)} %copy-done.3), kind=kOutput, calls=%fused_computation.49 | convolution fusion | flops 294973440 | bytes 2703872 | tf_op jit(solution)/shard_map/conv_general_dilated | solution.py:25
  29.7 0.2 fusion.39
  29.9 1.0 %fusion.27 = f32[4,16,3,320]{3,1,2,0:T(8,128)S(1)} fusion(bf16[2,320,3,3,320]{4,1,3,2,0:T(8,128)(2,1)S(1)} %maximum_select_fusion.1, bf16[4,2,8,5,320]{4,1,3,2,0:T(2,128)(2,1)S(1)} %fusion.39, pred[16,3]{0,1:T(4,128)(4,1)S(1)} %copy-done.3), kind=kOutput, calls=%fused_computation.47 | convolution fusion | flops 294973440 | bytes 2703872 | tf_op jit(solution)/shard_map/conv_general_dilated | solution.py:25
  31.2 0.1 rev.25
  31.7 0.2 fusion.40
  31.9 2.4 %fusion.28 = f32[4,16,3,320]{3,1,2,0:T(8,128)S(1)} fusion(bf16[2,320,3,3,320]{4,1,3,2,0:T(8,128)(2,1)} %copy-done, bf16[4,2,8,5,320]{4,1,3,2,0:T(2,128)(2,1)S(1)} %fusion.40, pred[16,3]{0,1:T(4,128)(4,1)S(1)} %copy-done.3), kind=kOutput, calls=%fused_computation.48 | convolution fusion | flops 294973440 | bytes 2662448 | tf_op jit(solution)/shard_map/conv_general_dilated | solution.py:37
  34.7 0.1 rev.27
  35.1 0.2 fusion.41
  35.4 2.4 %fusion.30 = f32[4,16,3,320]{3,1,2,0:T(8,128)S(1)} fusion(bf16[2,320,3,3,320]{4,1,3,2,0:T(8,128)(2,1)} %copy-done, bf16[4,2,8,5,320]{4,1,3,2,0:T(2,128)(2,1)S(1)} %fusion.41, pred[16,3]{0,1:T(4,128)(4,1)S(1)} %copy-done.3), kind=kOutput, calls=%fused_computation.50 | convolution fusion | flops 294973440 | bytes 2662448 | tf_op jit(solution)/shard_map/conv_general_dilated | solution.py:37
  38.0 0.2 fusion.75
  38.2 1.3 %collective-permute-start.3 = (bf16[2,4,16,320]{3,2,1,0:T(8,128)(2,1)S(1)}, bf16[2,4,16,320]{3,2,1,0:T(8,128)(2,1)S(1)}, u32[]{:S(2)}, u32[]{:S(2)}) collective-permute-start(bf16[2,4,16,320]{3,2,1,0:T(8,128)(2,1)S(1)} %fusion.75), channel_id=1, source_target_pairs={{4,0},{8,12},{5,1},{9,13},{6,2},{10,14},{7,3},{11,15},{20,16},{24,... | collective-permute-start | bytes 245768 | tf_op jit(solution)/shard_map/ppermute | solution.py:203
  39.5 5.2 %collective-permute-done.3 = bf16[2,4,16,320]{3,2,1,0:T(8,128)(2,1)S(1)} collective-permute-done((bf16[2,4,16,320]{3,2,1,0:T(8,128)(2,1)S(1)}, bf16[2,4,16,320]{3,2,1,0:T(8,128)(2,1)S(1)}, u32[]{:S(2)}, u32[]{:S(2)}) %collective-permute-start.3) | collective-permute-done | bytes 81952 | tf_op jit(solution)/shard_map/ppermute | solution.py:203
  44.7 0.2 fusion.82
  45.1 0.3 copy_dynamic-update-slice_fusion.3
  45.4 4.4 %collective-permute-done.4 = bf16[2,4,16,640]{3,2,1,0:T(8,128)(2,1)S(1)} collective-permute-done((bf16[2,4,16,640]{3,2,1,0:T(8,128)(2,1)S(1)}, bf16[2,4,16,640]{3,2,1,0:T(8,128)(2,1)S(1)}, u32[]{:S(2)}, u32[]{:S(2)}) %collective-permute-start.4) | collective-permute-done | bytes 163872 | tf_op jit(solution)/shard_map/ppermute | solution.py:14
  49.8 0.3 copy_dynamic-update-slice_fusion.2
  50.1 4.5 %collective-permute-done.5 = bf16[2,4,16,640]{3,2,1,0:T(8,128)(2,1)S(1)} collective-permute-done((bf16[2,4,16,640]{3,2,1,0:T(8,128)(2,1)S(1)}, bf16[2,4,16,640]{3,2,1,0:T(8,128)(2,1)S(1)}, u32[]{:S(2)}, u32[]{:S(2)}) %collective-permute-start.5) | collective-permute-done | bytes 163872 | tf_op jit(solution)/shard_map/ppermute | solution.py:14
  54.5 0.3 copy_dynamic-update-slice_fusion.1
  54.8 4.5 %collective-permute-done.6 = bf16[2,4,16,640]{3,2,1,0:T(8,128)(2,1)S(1)} collective-permute-done((bf16[2,4,16,640]{3,2,1,0:T(8,128)(2,1)S(1)}, bf16[2,4,16,640]{3,2,1,0:T(8,128)(2,1)S(1)}, u32[]{:S(2)}, u32[]{:S(2)}) %collective-permute-start.6) | collective-permute-done | bytes 163872 | tf_op jit(solution)/shard_map/ppermute | solution.py:14
  59.3 0.3 copy_dynamic-update-slice_fusion
  59.6 0.9 %fusion.35 = f32[160,3,3,320]{3,0,2,1:T(8,128)S(1)} fusion(bf16[8,4,16,640]{3,0,2,1:T(8,128)(2,1)S(1)} %copy_dynamic-update-slice_fusion, s32[]{:T(128)S(6)} %select_n.105), kind=kOutput, calls=%fused_computation.56 | convolution fusion | flops 376832000 | bytes 2498564 | tf_op jit(solution)/shard_map/conv_general_dilated | solution.py:60
  60.5 1.5 %copy.132 = f32[160,3,3,320]{3,2,1,0:T(4,128)S(1)} copy(f32[160,3,3,320]{3,0,2,1:T(8,128)S(1)} %fusion.35) | data formatting | bytes 3686400 | tf_op jit(solution)/shard_map/conv_general_dilated | solution.py:60
  62.0 4.6 %reshape.19 = f32[1,460800]{1,0:T(1,128)} reshape(f32[160,3,3,320]{3,2,1,0:T(4,128)S(1)} %copy.132) | data formatting | bytes 3686400 | tf_op jit(solution)/shard_map/reshape | solution.py:217
  (72 shorter events, 4.3 us)
Async XLA Ops:
  7.1 3.2 %copy-start.1 = (bf16[1,2,2,4,16,320]{5,4,3,2,1,0:T(8,128)(2,1)S(1)}, bf16[1,2,2,4,16,320]{5,4,3,2,1,0:T(8,128)(2,1)}, u32[]{:S(2)}) copy-start(bf16[1,2,2,4,16,320]{5,4,3,2,1,0:T(8,128)(2,1)} %param.11) | copy-start | bytes 491524
  7.1 3.2 %copy-start.2 = (bf16[1,2,2,4,16,320]{5,4,3,2,1,0:T(8,128)(2,1)S(1)}, bf16[1,2,2,4,16,320]{5,4,3,2,1,0:T(8,128)(2,1)}, u32[]{:S(2)}) copy-start(bf16[1,2,2,4,16,320]{5,4,3,2,1,0:T(8,128)(2,1)} %param.9) | copy-start | bytes 491524
  9.8 4.6 %collective-permute-start = (bf16[2,160,3,3,320]{4,1,3,2,0:T(8,128)(2,1)S(1)}, bf16[2,160,3,3,320]{4,1,3,2,0:T(8,128)(2,1)}, u32[]{:S(2)}, u32[]{:S(2)}) collective-permute-start(bf16[2,160,3,3,320]{4,1,3,2,0:T(8,128)(2,1)S(1)} %bitcast.137), channel_id=1, source_target_pairs={{0,1},{1,0},{2,3},{3,2},{4,5},{5,4},{6,7},{7,6},{8,9},{9,8},{10,11... | collective-permute-start | bytes 5529608 | tf_op jit(solution)/shard_map/ppermute | solution.py:109
  11.1 1.9 %copy-start.4 = (pred[16,3]{0,1:T(4,128)(4,1)S(1)}, pred[16,3]{0,1:T(4,128)(4,1)}, u32[]{:S(2)}) copy-start(pred[16,3]{0,1:T(4,128)(4,1)} %constant.125) | copy-start | bytes 148 | tf_op jit(solution)/shard_map/cond
  17.1 10.3 %collective-permute-start.1 = (bf16[2,4,16,320]{3,2,1,0:T(8,128)(2,1)S(1)}, bf16[2,4,16,320]{3,2,1,0:T(8,128)(2,1)S(1)}, u32[]{:S(2)}, u32[]{:S(2)}) collective-permute-start(bf16[2,4,16,320]{3,2,1,0:T(8,128)(2,1)S(1)} %copy.109), channel_id=1, source_target_pairs={{0,4},{12,8},{1,5},{13,9},{2,6},{14,10},{3,7},{15,11},{16,20},{28,... | collective-permute-start | bytes 245768 | tf_op jit(solution)/shard_map/ppermute | solution.py:113
  22.3 5.7 %copy-start.3 = (pred[16,3]{0,1:T(4,128)(4,1)S(1)}, pred[16,3]{0,1:T(4,128)(4,1)}, u32[]{:S(2)}) copy-start(pred[16,3]{0,1:T(4,128)(4,1)} %constant.119) | copy-start | bytes 148
  22.3 8.7 %collective-permute-start.2 = (f32[2,4,16,320]{3,2,1,0:T(8,128)S(1)}, f32[2,4,16,320]{3,2,1,0:T(8,128)S(1)}, u32[]{:S(2)}, u32[]{:S(2)}) collective-permute-start(f32[2,4,16,320]{3,2,1,0:T(8,128)S(1)} %copy.111), channel_id=1, source_target_pairs={{0,4},{12,8},{1,5},{13,9},{2,6},{14,10},{3,7},{15,11},{16,20},{28,... | collective-permute-start | bytes 491528 | tf_op jit(solution)/shard_map/ppermute | solution.py:113
  27.4 2.5 %copy-start = (bf16[2,320,3,3,320]{4,1,3,2,0:T(8,128)(2,1)}, bf16[2,320,3,3,320]{4,1,3,2,0:T(8,128)(2,1)S(1)}, u32[]{:S(2)}) copy-start(bf16[2,320,3,3,320]{4,1,3,2,0:T(8,128)(2,1)S(1)} %maximum_select_fusion.1) | copy-start | bytes 11059204
  38.2 6.5 %collective-permute-start.3 = (bf16[2,4,16,320]{3,2,1,0:T(8,128)(2,1)S(1)}, bf16[2,4,16,320]{3,2,1,0:T(8,128)(2,1)S(1)}, u32[]{:S(2)}, u32[]{:S(2)}) collective-permute-start(bf16[2,4,16,320]{3,2,1,0:T(8,128)(2,1)S(1)} %fusion.75), channel_id=1, source_target_pairs={{4,0},{8,12},{5,1},{9,13},{6,2},{10,14},{7,3},{11,15},{20,16},{24,... | collective-permute-start | bytes 245768 | tf_op jit(solution)/shard_map/ppermute | solution.py:203
  45.0 4.8 %collective-permute-start.4 = (bf16[2,4,16,640]{3,2,1,0:T(8,128)(2,1)S(1)}, bf16[2,4,16,640]{3,2,1,0:T(8,128)(2,1)S(1)}, u32[]{:S(2)}, u32[]{:S(2)}) collective-permute-start(bf16[2,4,16,640]{3,2,1,0:T(8,128)(2,1)S(1)} %pad_maximum_fusion), channel_id=1, source_target_pairs={{0,1},{1,2},{2,3},{3,0},{4,5},{5,6},{6,7},{7,4},{8,9},{9,10},{10,1... | collective-permute-start | bytes 491528 | tf_op jit(solution)/shard_map/ppermute | solution.py:14
  49.8 4.7 %collective-permute-start.5 = (bf16[2,4,16,640]{3,2,1,0:T(8,128)(2,1)S(1)}, bf16[2,4,16,640]{3,2,1,0:T(8,128)(2,1)S(1)}, u32[]{:S(2)}, u32[]{:S(2)}) collective-permute-start(bf16[2,4,16,640]{3,2,1,0:T(8,128)(2,1)S(1)} %collective-permute-done.4), channel_id=1, source_target_pairs={{0,1},{1,2},{2,3},{3,0},{4,5},{5,6},{6,7},{7,4},{8,9},{9,10},{10,1... | collective-permute-start | bytes 491528 | tf_op jit(solution)/shard_map/ppermute | solution.py:14
  54.5 4.7 %collective-permute-start.6 = (bf16[2,4,16,640]{3,2,1,0:T(8,128)(2,1)S(1)}, bf16[2,4,16,640]{3,2,1,0:T(8,128)(2,1)S(1)}, u32[]{:S(2)}, u32[]{:S(2)}) collective-permute-start(bf16[2,4,16,640]{3,2,1,0:T(8,128)(2,1)S(1)} %collective-permute-done.5), channel_id=1, source_target_pairs={{0,1},{1,2},{2,3},{3,0},{4,5},{5,6},{6,7},{7,4},{8,9},{9,10},{10,1... | collective-permute-start | bytes 491528 | tf_op jit(solution)/shard_map/ppermute | solution.py:14
